TPU v7x, 32 devices: a whole 2x2x4 slice. The times are simulated.
32 devices in a mesh: groups: 2 (over y), space: 4 (over z), blk: 2 (over x), samp: 2 (over core).
Axes of the slice: x: 2, y: 2, z: 4, core: 2. Of those that a mesh axis runs over, the one named last changes fastest.
Arguments:
- coeff: bfloat16 [16, 4, 512, 512], P(('groups', 'space', 'blk')), parts along dimension 0, may hold values from -0.125 to 0.125
- solve: bfloat16 [16, 512, 512], P(('groups', 'space', 'blk')), parts along dimension 0
- noise: float32 [16, 512, 512], P(('groups', 'space', 'blk'), 'samp'), parts along dimension 0, may hold values from -6 to 6
- prior: bfloat16 [16, 512, 512], P(('groups', 'space', 'blk'), 'samp'), parts along dimension 0, may hold values from -6 to 6
- owner: int32 [16], P('groups'), parts along dimension 0, may hold values from 0 to 7, as said below
- nbrs: int32 [16, 4], P('groups'), parts along dimension 0, may hold values from 0 to 15, as said below
Outputs:
- field: bfloat16 [16, 512, 512], P(('groups', 'space', 'blk'), 'samp'), parts along dimension 0
There are 2 independent parts, one for each index of `groups`. A program takes and returns all parts, laid end to end along the dimension named above; each array names one. Nothing has to cross between parts.
Inputs may be any that keep to these rules, and one draw needn't show every extreme that they name: `owner`: A permutation of the blocks. `nbrs`: the 4 entries of a block are distinct. An entry v < 8 names block v's prior field; v >= 8 names the field of block v - 8; these references form no cycle, and every chain of them holds at most 4 blocks. The slot of every named block lies in a partition (slot // 2) at most 1 away from the reader's partition.
All inputs are finite; a program needn't handle non-finite values.
Results may differ from a plain program's by a relative error of at most 0.0056.
Values may be sent and summed in bfloat16 or wider, within the bound.
No kernel may reach another device: no remote copies, remote signals or barrier semaphores. Data moves between devices by JAX's collectives and lax.ppermute only.
A program may use at most 64 MiB of HBM per device.

v0:
```python
import jax
import jax.numpy as jnp
from jax import lax
from jax.sharding import PartitionSpec as P

LEVELS = 4
REACH = 1


def block_levels(nbrs, count):
    block_ids = jnp.arange(count, dtype=jnp.int32)
    is_current = nbrs >= count
    target = jnp.remainder(nbrs, count)
    picks = target[:, :, None] == block_ids[None, None, :]
    levels = jnp.zeros((count,), jnp.int32)
    for sweep in range(LEVELS):
        looked = jnp.sum(jnp.where(picks, levels[None, None, :], 0), axis=2)
        above = jnp.where(is_current, looked + 1, 0)
        levels = jnp.max(above, axis=1)
    return levels


def window_pairs(space_count, part_size, distance, offset):
    pairs = []
    for space_to in range(space_count):
        space_from = space_to + distance
        if not 0 <= space_from < space_count:
            continue
        for blk_to in range(part_size):
            blk_from = (blk_to + offset) % part_size
            pairs.append((space_from * part_size + blk_from, space_to * part_size + blk_to))
    return pairs


def neighbourhood(local_block):
    part_size = lax.axis_size("blk")
    space_count = lax.axis_size("space")
    pieces = []
    for distance in range(-REACH, REACH + 1):
        for offset in range(part_size):
            if distance == 0 and offset == 0:
                pieces.append(local_block)
                continue
            pairs = window_pairs(space_count, part_size, distance, offset)
            pieces.append(lax.ppermute(local_block, ("space", "blk"), pairs))
    return jnp.stack(pieces, axis=0)


def body(coeff, solve, noise, prior, owner, nbrs):
    part_size = lax.axis_size("blk")
    space_index = lax.axis_index("space")
    blk_index = lax.axis_index("blk")
    own_slot = space_index * part_size + blk_index
    count = owner.shape[0]
    neigh = nbrs.shape[1]
    block_ids = jnp.arange(count, dtype=jnp.int32)
    levels = block_levels(nbrs, count)
    own_block = jnp.sum(jnp.where(owner == own_slot, block_ids, 0))
    own_level = jnp.sum(jnp.where(block_ids == own_block, levels, 0))
    own_list = jnp.sum(jnp.where((block_ids == own_block)[:, None], nbrs, 0), axis=0)
    is_current = own_list >= count
    target = jnp.remainder(own_list, count)
    near_slot = jnp.sum(jnp.where(target[:, None] == block_ids[None, :], owner[None, :], 0), axis=1)
    distance = near_slot // part_size - space_index
    offset = jnp.remainder(near_slot - blk_index, part_size)
    piece = (distance + REACH) * part_size + offset

    prior_window = neighbourhood(prior[0])
    start = noise[0]
    for j in range(neigh):
        values = lax.dynamic_index_in_dim(prior_window, piece[j], 0, keepdims=False)
        term = jnp.dot(values, coeff[0, j], preferred_element_type=jnp.float32)
        start = start - jnp.where(is_current[j], jnp.zeros_like(term), term)

    current = jnp.zeros_like(prior[0])
    window = None
    for level_now in range(LEVELS):

        def compute_block(previous, window_now=window):
            right_side = start
            if window_now is not None:
                for j in range(neigh):
                    values = lax.dynamic_index_in_dim(window_now, piece[j], 0, keepdims=False)
                    term = jnp.dot(values, coeff[0, j], preferred_element_type=jnp.float32)
                    right_side = right_side - jnp.where(is_current[j], term, jnp.zeros_like(term))
            result = jnp.dot(right_side.astype(jnp.bfloat16), solve[0], preferred_element_type=jnp.float32)
            return result.astype(jnp.bfloat16)

        def unchanged(previous):
            return previous

        current = lax.cond(own_level == level_now, compute_block, unchanged, current)
        if level_now + 1 < LEVELS:
            window = neighbourhood(current)
    return current[None]


def solution(mesh):
    placed = (
        P(("groups", "space", "blk"), None, None, None),
        P(("groups", "space", "blk"), None, None),
        P(("groups", "space", "blk"), "samp", None),
        P(("groups", "space", "blk"), "samp", None),
        P("groups"),
        P("groups", None),
    )
    return jax.shard_map(
        body,
        mesh=mesh,
        in_specs=placed,
        out_specs=P(("groups", "space", "blk"), "samp", None),
        check_vma=False,
    )
```

profile of v0, /device:TPU:12, one launch (start us, length us, event | category | flops | bytes accessed | tf_op | source)
XLA Modules:
  0.0 149.8 jit_solution(6541506068735028741)
XLA Ops:
  0.0 3.5 %collective-permute-start = (bf16[256,512]{1,0:T(8,128)(2,1)}, bf16[256,512]{1,0:T(8,128)(2,1)S(1)}, u32[]{:S(2)}, u32[]{:S(2)}) collective-permute-start(bf16[256,512]{1,0:T(8,128)(2,1)} %bitcast.199), channel_id=1, source_target_pairs={{0,4},{2,6},{4,8},{6,10},{8,12},{10,14},{1,5},{3,7},{5,9},{7,11},{... | collective-permute-start | bytes 786440 | tf_op jit(solution)/shard_map/ppermute | solution.py:45
  3.5 4.4 %collective-permute-start.1 = (bf16[256,512]{1,0:T(8,128)(2,1)}, bf16[256,512]{1,0:T(8,128)(2,1)S(1)}, u32[]{:S(2)}, u32[]{:S(2)}) collective-permute-start(bf16[256,512]{1,0:T(8,128)(2,1)} %bitcast.200), channel_id=1, source_target_pairs={{2,4},{0,6},{6,8},{4,10},{10,12},{8,14},{3,5},{1,7},{7,9},{5,11},{... | collective-permute-start | bytes 786440 | tf_op jit(solution)/shard_map/ppermute | solution.py:45
  8.5 2.4 %collective-permute-start.3 = (bf16[256,512]{1,0:T(8,128)(2,1)}, bf16[256,512]{1,0:T(8,128)(2,1)S(1)}, u32[]{:S(2)}, u32[]{:S(2)}) collective-permute-start(bf16[256,512]{1,0:T(8,128)(2,1)} %bitcast.202), channel_id=1, source_target_pairs={{4,0},{6,2},{8,4},{10,6},{12,8},{14,10},{5,1},{7,3},{9,5},{11,7},{... | collective-permute-start | bytes 786440 | tf_op jit(solution)/shard_map/ppermute | solution.py:45
  10.9 2.2 %collective-permute-start.4 = (bf16[256,512]{1,0:T(8,128)(2,1)}, bf16[256,512]{1,0:T(8,128)(2,1)S(1)}, u32[]{:S(2)}, u32[]{:S(2)}) collective-permute-start(bf16[256,512]{1,0:T(8,128)(2,1)} %bitcast.203), channel_id=1, source_target_pairs={{6,0},{4,2},{10,4},{8,6},{14,8},{12,10},{7,1},{5,3},{11,5},{9,7},{... | collective-permute-start | bytes 786440 | tf_op jit(solution)/shard_map/ppermute | solution.py:45
  13.1 1.3 fusion.131
  15.1 0.8 select_reduce_fusion.8
  15.9 0.8 select_reduce_fusion.3
  18.8 1.4 select_reduce_fusion.9
  28.5 1.1 constant_dynamic-update-slice_fusion
  30.1 0.9 fusion.108
  31.1 0.9 fusion.107
  32.0 1.0 fusion.106
  33.0 0.9 fusion.105
  34.2 4.3 %collective-permute-start.5 = (bf16[256,512]{1,0:T(8,128)(2,1)S(1)}, bf16[256,512]{1,0:T(8,128)(2,1)}, u32[]{:S(2)}, u32[]{:S(2)}) collective-permute-start(bf16[256,512]{1,0:T(8,128)(2,1)S(1)} %get-tuple-element.121), channel_id=1, source_target_pairs={{0,4},{2,6},{4,8},{6,10},{8,12},{10,14},{1,5},{3,7},{5,9},{7,11},{... | collective-permute-start | bytes 786440 | tf_op jit(solution)/shard_map/ppermute | solution.py:45
  38.5 3.5 %collective-permute-start.6 = (bf16[256,512]{1,0:T(8,128)(2,1)S(1)}, bf16[256,512]{1,0:T(8,128)(2,1)}, u32[]{:S(2)}, u32[]{:S(2)}) collective-permute-start(bf16[256,512]{1,0:T(8,128)(2,1)S(1)} %get-tuple-element.121), channel_id=1, source_target_pairs={{2,4},{0,6},{6,8},{4,10},{10,12},{8,14},{3,5},{1,7},{7,9},{5,11},{... | collective-permute-start | bytes 786440 | tf_op jit(solution)/shard_map/ppermute | solution.py:45
  42.7 1.8 %collective-permute-start.7 = (bf16[256,512]{1,0:T(8,128)(2,1)S(1)}, bf16[256,512]{1,0:T(8,128)(2,1)S(1)}, u32[]{:S(2)}, u32[]{:S(2)}) collective-permute-start(bf16[256,512]{1,0:T(8,128)(2,1)S(1)} %get-tuple-element.121), channel_id=1, source_target_pairs={{2,0},{0,2},{6,4},{4,6},{10,8},{8,10},{14,12},{12,14},{3,1},{1,3},... | collective-permute-start | bytes 786440 | tf_op jit(solution)/shard_map/ppermute | solution.py:45
  44.5 2.8 %collective-permute-start.8 = (bf16[256,512]{1,0:T(8,128)(2,1)S(1)}, bf16[256,512]{1,0:T(8,128)(2,1)S(1)}, u32[]{:S(2)}, u32[]{:S(2)}) collective-permute-start(bf16[256,512]{1,0:T(8,128)(2,1)S(1)} %get-tuple-element.121), channel_id=1, source_target_pairs={{4,0},{6,2},{8,4},{10,6},{12,8},{14,10},{5,1},{7,3},{9,5},{11,7},{... | collective-permute-start | bytes 786440 | tf_op jit(solution)/shard_map/ppermute | solution.py:45
  47.3 1.9 %collective-permute-start.9 = (bf16[256,512]{1,0:T(8,128)(2,1)S(1)}, bf16[256,512]{1,0:T(8,128)(2,1)S(1)}, u32[]{:S(2)}, u32[]{:S(2)}) collective-permute-start(bf16[256,512]{1,0:T(8,128)(2,1)S(1)} %get-tuple-element.121), channel_id=1, source_target_pairs={{6,0},{4,2},{10,4},{8,6},{14,8},{12,10},{7,1},{5,3},{11,5},{9,7},{... | collective-permute-start | bytes 786440 | tf_op jit(solution)/shard_map/ppermute | solution.py:45
  49.2 1.7 %bitcast_dynamic-update-slice_fusion.17 = bf16[6,256,512]{2,1,0:T(8,128)(2,1)} fusion(bf16[256,512]{1,0:T(8,128)(2,1)} %collective-permute-done.5), kind=kLoop, calls=%fused_computation.139 | loop fusion | bytes 524288
  50.9 1.7 %bitcast_dynamic-update-slice_fusion.16 = bf16[6,256,512]{2,1,0:T(8,128)(2,1)} fusion(bf16[6,256,512]{2,1,0:T(8,128)(2,1)} %bitcast_dynamic-update-slice_fusion.17, bf16[256,512]{1,0:T(8,128)(2,1)} %collective-permute-done.6), kind=kLoop, calls=%fused_computation.138 | loop fusion | bytes 524288
  52.5 0.7 bitcast_dynamic-update-slice_fusion.15
  53.3 6.3 %collective-permute-done.7 = bf16[256,512]{1,0:T(8,128)(2,1)S(1)} collective-permute-done((bf16[256,512]{1,0:T(8,128)(2,1)S(1)}, bf16[256,512]{1,0:T(8,128)(2,1)S(1)}, u32[]{:S(2)}, u32[]{:S(2)}) %collective-permute-start.7) | collective-permute-done | bytes 262176 | tf_op jit(solution)/shard_map/ppermute | solution.py:45
  60.2 0.7 bitcast_dynamic-update-slice_fusion.13
  61.0 0.7 bitcast_dynamic-update-slice_fusion.12
  61.7 21.1 %collective-permute-start.10 = (bf16[256,512]{1,0:T(8,128)(2,1)S(1)}, bf16[256,512]{1,0:T(8,128)(2,1)S(1)}, u32[]{:S(2)}, u32[]{:S(2)}) collective-permute-start(bf16[256,512]{1,0:T(8,128)(2,1)S(1)} %get-tuple-element.122), channel_id=1, source_target_pairs={{0,4},{2,6},{4,8},{6,10},{8,12},{10,14},{1,5},{3,7},{5,9},{7,11},{... | collective-permute-start | bytes 786440 | tf_op jit(solution)/shard_map/ppermute | solution.py:45
  82.8 1.9 %collective-permute-start.11 = (bf16[256,512]{1,0:T(8,128)(2,1)S(1)}, bf16[256,512]{1,0:T(8,128)(2,1)S(1)}, u32[]{:S(2)}, u32[]{:S(2)}) collective-permute-start(bf16[256,512]{1,0:T(8,128)(2,1)S(1)} %get-tuple-element.122), channel_id=1, source_target_pairs={{2,4},{0,6},{6,8},{4,10},{10,12},{8,14},{3,5},{1,7},{7,9},{5,11},{... | collective-permute-start | bytes 786440 | tf_op jit(solution)/shard_map/ppermute | solution.py:45
  85.4 1.5 %collective-permute-start.12 = (bf16[256,512]{1,0:T(8,128)(2,1)S(1)}, bf16[256,512]{1,0:T(8,128)(2,1)S(1)}, u32[]{:S(2)}, u32[]{:S(2)}) collective-permute-start(bf16[256,512]{1,0:T(8,128)(2,1)S(1)} %get-tuple-element.122), channel_id=1, source_target_pairs={{2,0},{0,2},{6,4},{4,6},{10,8},{8,10},{14,12},{12,14},{3,1},{1,3},... | collective-permute-start | bytes 786440 | tf_op jit(solution)/shard_map/ppermute | solution.py:45
  87.0 3.9 %collective-permute-start.13 = (bf16[256,512]{1,0:T(8,128)(2,1)S(1)}, bf16[256,512]{1,0:T(8,128)(2,1)S(1)}, u32[]{:S(2)}, u32[]{:S(2)}) collective-permute-start(bf16[256,512]{1,0:T(8,128)(2,1)S(1)} %get-tuple-element.122), channel_id=1, source_target_pairs={{4,0},{6,2},{8,4},{10,6},{12,8},{14,10},{5,1},{7,3},{9,5},{11,7},{... | collective-permute-start | bytes 786440 | tf_op jit(solution)/shard_map/ppermute | solution.py:45
  90.9 1.9 %collective-permute-start.14 = (bf16[256,512]{1,0:T(8,128)(2,1)S(1)}, bf16[256,512]{1,0:T(8,128)(2,1)S(1)}, u32[]{:S(2)}, u32[]{:S(2)}) collective-permute-start(bf16[256,512]{1,0:T(8,128)(2,1)S(1)} %get-tuple-element.122), channel_id=1, source_target_pairs={{6,0},{4,2},{10,4},{8,6},{14,8},{12,10},{7,1},{5,3},{11,5},{9,7},{... | collective-permute-start | bytes 786440 | tf_op jit(solution)/shard_map/ppermute | solution.py:45
  92.8 0.7 bitcast_dynamic-update-slice_fusion.11
  93.6 0.7 bitcast_dynamic-update-slice_fusion.10
  94.3 0.7 bitcast_dynamic-update-slice_fusion.9
  95.0 8.3 %collective-permute-done.12 = bf16[256,512]{1,0:T(8,128)(2,1)S(1)} collective-permute-done((bf16[256,512]{1,0:T(8,128)(2,1)S(1)}, bf16[256,512]{1,0:T(8,128)(2,1)S(1)}, u32[]{:S(2)}, u32[]{:S(2)}) %collective-permute-start.12) | collective-permute-done | bytes 262176 | tf_op jit(solution)/shard_map/ppermute | solution.py:45
  103.3 0.7 bitcast_dynamic-update-slice_fusion.8
  104.0 0.7 bitcast_dynamic-update-slice_fusion.7
  104.8 0.7 bitcast_dynamic-update-slice_fusion.6
  105.5 2.2 %collective-permute-start.15 = (bf16[256,512]{1,0:T(8,128)(2,1)S(1)}, bf16[256,512]{1,0:T(8,128)(2,1)S(1)}, u32[]{:S(2)}, u32[]{:S(2)}) collective-permute-start(bf16[256,512]{1,0:T(8,128)(2,1)S(1)} %get-tuple-element.123), channel_id=1, source_target_pairs={{0,4},{2,6},{4,8},{6,10},{8,12},{10,14},{1,5},{3,7},{5,9},{7,11},{... | collective-permute-start | bytes 786440 | tf_op jit(solution)/shard_map/ppermute | solution.py:45
  107.7 20.1 %collective-permute-start.16 = (bf16[256,512]{1,0:T(8,128)(2,1)S(1)}, bf16[256,512]{1,0:T(8,128)(2,1)S(1)}, u32[]{:S(2)}, u32[]{:S(2)}) collective-permute-start(bf16[256,512]{1,0:T(8,128)(2,1)S(1)} %get-tuple-element.123), channel_id=1, source_target_pairs={{2,4},{0,6},{6,8},{4,10},{10,12},{8,14},{3,5},{1,7},{7,9},{5,11},{... | collective-permute-start | bytes 786440 | tf_op jit(solution)/shard_map/ppermute | solution.py:45
  129.1 3.4 %collective-permute-start.18 = (bf16[256,512]{1,0:T(8,128)(2,1)S(1)}, bf16[256,512]{1,0:T(8,128)(2,1)S(1)}, u32[]{:S(2)}, u32[]{:S(2)}) collective-permute-start(bf16[256,512]{1,0:T(8,128)(2,1)S(1)} %get-tuple-element.123), channel_id=1, source_target_pairs={{4,0},{6,2},{8,4},{10,6},{12,8},{14,10},{5,1},{7,3},{9,5},{11,7},{... | collective-permute-start | bytes 786440 | tf_op jit(solution)/shard_map/ppermute | solution.py:45
  132.5 2.7 %collective-permute-start.19 = (bf16[256,512]{1,0:T(8,128)(2,1)S(1)}, bf16[256,512]{1,0:T(8,128)(2,1)S(1)}, u32[]{:S(2)}, u32[]{:S(2)}) collective-permute-start(bf16[256,512]{1,0:T(8,128)(2,1)S(1)} %get-tuple-element.123), channel_id=1, source_target_pairs={{6,0},{4,2},{10,4},{8,6},{14,8},{12,10},{7,1},{5,3},{11,5},{9,7},{... | collective-permute-start | bytes 786440 | tf_op jit(solution)/shard_map/ppermute | solution.py:45
  135.3 0.7 bitcast_dynamic-update-slice_fusion.5
  136.0 4.2 %collective-permute-done.16 = bf16[256,512]{1,0:T(8,128)(2,1)S(1)} collective-permute-done((bf16[256,512]{1,0:T(8,128)(2,1)S(1)}, bf16[256,512]{1,0:T(8,128)(2,1)S(1)}, u32[]{:S(2)}, u32[]{:S(2)}) %collective-permute-start.16) | collective-permute-done | bytes 262176 | tf_op jit(solution)/shard_map/ppermute | solution.py:45
  140.2 0.7 bitcast_dynamic-update-slice_fusion.4
  140.9 0.7 bitcast_dynamic-update-slice_fusion.3
  141.7 5.3 %collective-permute-done.17 = bf16[256,512]{1,0:T(8,128)(2,1)S(1)} collective-permute-done((bf16[256,512]{1,0:T(8,128)(2,1)S(1)}, bf16[256,512]{1,0:T(8,128)(2,1)S(1)}, u32[]{:S(2)}, u32[]{:S(2)}) %collective-permute-start.17) | collective-permute-done | bytes 262176 | tf_op jit(solution)/shard_map/ppermute | solution.py:45
  146.9 0.7 bitcast_dynamic-update-slice_fusion.2
  147.6 0.7 bitcast_dynamic-update-slice_fusion.1
  148.4 0.7 bitcast_dynamic-update-slice_fusion
  (49 shorter events, 6.5 us)
Async XLA Ops:
  0.0 28.4 %collective-permute-start = (bf16[256,512]{1,0:T(8,128)(2,1)}, bf16[256,512]{1,0:T(8,128)(2,1)S(1)}, u32[]{:S(2)}, u32[]{:S(2)}) collective-permute-start(bf16[256,512]{1,0:T(8,128)(2,1)} %bitcast.199), channel_id=1, source_target_pairs={{0,4},{2,6},{4,8},{6,10},{8,12},{10,14},{1,5},{3,7},{5,9},{7,11},{... | collective-permute-start | bytes 786440 | tf_op jit(solution)/shard_map/ppermute | solution.py:45
  3.5 25.0 %collective-permute-start.1 = (bf16[256,512]{1,0:T(8,128)(2,1)}, bf16[256,512]{1,0:T(8,128)(2,1)S(1)}, u32[]{:S(2)}, u32[]{:S(2)}) collective-permute-start(bf16[256,512]{1,0:T(8,128)(2,1)} %bitcast.200), channel_id=1, source_target_pairs={{2,4},{0,6},{6,8},{4,10},{10,12},{8,14},{3,5},{1,7},{7,9},{5,11},{... | collective-permute-start | bytes 786440 | tf_op jit(solution)/shard_map/ppermute | solution.py:45
  7.9 21.7 %collective-permute-start.2 = (bf16[256,512]{1,0:T(8,128)(2,1)}, bf16[256,512]{1,0:T(8,128)(2,1)S(1)}, u32[]{:S(2)}, u32[]{:S(2)}) collective-permute-start(bf16[256,512]{1,0:T(8,128)(2,1)} %bitcast.201), channel_id=1, source_target_pairs={{2,0},{0,2},{6,4},{4,6},{10,8},{8,10},{14,12},{12,14},{3,1},{1,3},... | collective-permute-start | bytes 786440 | tf_op jit(solution)/shard_map/ppermute | solution.py:45
  8.5 21.1 %collective-permute-start.3 = (bf16[256,512]{1,0:T(8,128)(2,1)}, bf16[256,512]{1,0:T(8,128)(2,1)S(1)}, u32[]{:S(2)}, u32[]{:S(2)}) collective-permute-start(bf16[256,512]{1,0:T(8,128)(2,1)} %bitcast.202), channel_id=1, source_target_pairs={{4,0},{6,2},{8,4},{10,6},{12,8},{14,10},{5,1},{7,3},{9,5},{11,7},{... | collective-permute-start | bytes 786440 | tf_op jit(solution)/shard_map/ppermute | solution.py:45
  10.9 18.8 %collective-permute-start.4 = (bf16[256,512]{1,0:T(8,128)(2,1)}, bf16[256,512]{1,0:T(8,128)(2,1)S(1)}, u32[]{:S(2)}, u32[]{:S(2)}) collective-permute-start(bf16[256,512]{1,0:T(8,128)(2,1)} %bitcast.203), channel_id=1, source_target_pairs={{6,0},{4,2},{10,4},{8,6},{14,8},{12,10},{7,1},{5,3},{11,5},{9,7},{... | collective-permute-start | bytes 786440 | tf_op jit(solution)/shard_map/ppermute | solution.py:45
  28.4 1.7 %copy-start = (bf16[1,4,512,512]{3,2,1,0:T(8,128)(2,1)S(1)}, bf16[1,4,512,512]{3,2,1,0:T(8,128)(2,1)}, u32[]{:S(2)}) copy-start(bf16[1,4,512,512]{3,2,1,0:T(8,128)(2,1)} %param.14) | copy-start | bytes 6291460
  28.4 1.7 %copy-start.2 = (f32[1,256,512]{2,1,0:T(8,128)S(1)}, f32[1,256,512]{2,1,0:T(8,128)}, u32[]{:S(2)}) copy-start(f32[1,256,512]{2,1,0:T(8,128)} %param.16) | copy-start | bytes 1572868
  32.0 1.9 %copy-start.3 = (bf16[1,512,512]{2,1,0:T(8,128)(2,1)S(1)}, bf16[1,512,512]{2,1,0:T(8,128)(2,1)}, u32[]{:S(2)}) copy-start(bf16[1,512,512]{2,1,0:T(8,128)(2,1)} %param.15) | copy-start | bytes 1572868
  34.2 15.0 %collective-permute-start.5 = (bf16[256,512]{1,0:T(8,128)(2,1)S(1)}, bf16[256,512]{1,0:T(8,128)(2,1)}, u32[]{:S(2)}, u32[]{:S(2)}) collective-permute-start(bf16[256,512]{1,0:T(8,128)(2,1)S(1)} %get-tuple-element.121), channel_id=1, source_target_pairs={{0,4},{2,6},{4,8},{6,10},{8,12},{10,14},{1,5},{3,7},{5,9},{7,11},{... | collective-permute-start | bytes 786440 | tf_op jit(solution)/shard_map/ppermute | solution.py:45
  38.5 12.4 %collective-permute-start.6 = (bf16[256,512]{1,0:T(8,128)(2,1)S(1)}, bf16[256,512]{1,0:T(8,128)(2,1)}, u32[]{:S(2)}, u32[]{:S(2)}) collective-permute-start(bf16[256,512]{1,0:T(8,128)(2,1)S(1)} %get-tuple-element.121), channel_id=1, source_target_pairs={{2,4},{0,6},{6,8},{4,10},{10,12},{8,14},{3,5},{1,7},{7,9},{5,11},{... | collective-permute-start | bytes 786440 | tf_op jit(solution)/shard_map/ppermute | solution.py:45
  42.7 16.9 %collective-permute-start.7 = (bf16[256,512]{1,0:T(8,128)(2,1)S(1)}, bf16[256,512]{1,0:T(8,128)(2,1)S(1)}, u32[]{:S(2)}, u32[]{:S(2)}) collective-permute-start(bf16[256,512]{1,0:T(8,128)(2,1)S(1)} %get-tuple-element.121), channel_id=1, source_target_pairs={{2,0},{0,2},{6,4},{4,6},{10,8},{8,10},{14,12},{12,14},{3,1},{1,3},... | collective-permute-start | bytes 786440 | tf_op jit(solution)/shard_map/ppermute | solution.py:45
  44.5 15.7 %collective-permute-start.8 = (bf16[256,512]{1,0:T(8,128)(2,1)S(1)}, bf16[256,512]{1,0:T(8,128)(2,1)S(1)}, u32[]{:S(2)}, u32[]{:S(2)}) collective-permute-start(bf16[256,512]{1,0:T(8,128)(2,1)S(1)} %get-tuple-element.121), channel_id=1, source_target_pairs={{4,0},{6,2},{8,4},{10,6},{12,8},{14,10},{5,1},{7,3},{9,5},{11,7},{... | collective-permute-start | bytes 786440 | tf_op jit(solution)/shard_map/ppermute | solution.py:45
  47.3 13.7 %collective-permute-start.9 = (bf16[256,512]{1,0:T(8,128)(2,1)S(1)}, bf16[256,512]{1,0:T(8,128)(2,1)S(1)}, u32[]{:S(2)}, u32[]{:S(2)}) collective-permute-start(bf16[256,512]{1,0:T(8,128)(2,1)S(1)} %get-tuple-element.121), channel_id=1, source_target_pairs={{6,0},{4,2},{10,4},{8,6},{14,8},{12,10},{7,1},{5,3},{11,5},{9,7},{... | collective-permute-start | bytes 786440 | tf_op jit(solution)/shard_map/ppermute | solution.py:45
  61.7 31.2 %collective-permute-start.10 = (bf16[256,512]{1,0:T(8,128)(2,1)S(1)}, bf16[256,512]{1,0:T(8,128)(2,1)S(1)}, u32[]{:S(2)}, u32[]{:S(2)}) collective-permute-start(bf16[256,512]{1,0:T(8,128)(2,1)S(1)} %get-tuple-element.122), channel_id=1, source_target_pairs={{0,4},{2,6},{4,8},{6,10},{8,12},{10,14},{1,5},{3,7},{5,9},{7,11},{... | collective-permute-start | bytes 786440 | tf_op jit(solution)/shard_map/ppermute | solution.py:45
  82.8 10.7 %collective-permute-start.11 = (bf16[256,512]{1,0:T(8,128)(2,1)S(1)}, bf16[256,512]{1,0:T(8,128)(2,1)S(1)}, u32[]{:S(2)}, u32[]{:S(2)}) collective-permute-start(bf16[256,512]{1,0:T(8,128)(2,1)S(1)} %get-tuple-element.122), channel_id=1, source_target_pairs={{2,4},{0,6},{6,8},{4,10},{10,12},{8,14},{3,5},{1,7},{7,9},{5,11},{... | collective-permute-start | bytes 786440 | tf_op jit(solution)/shard_map/ppermute | solution.py:45
  85.4 17.9 %collective-permute-start.12 = (bf16[256,512]{1,0:T(8,128)(2,1)S(1)}, bf16[256,512]{1,0:T(8,128)(2,1)S(1)}, u32[]{:S(2)}, u32[]{:S(2)}) collective-permute-start(bf16[256,512]{1,0:T(8,128)(2,1)S(1)} %get-tuple-element.122), channel_id=1, source_target_pairs={{2,0},{0,2},{6,4},{4,6},{10,8},{8,10},{14,12},{12,14},{3,1},{1,3},... | collective-permute-start | bytes 786440 | tf_op jit(solution)/shard_map/ppermute | solution.py:45
  87.0 17.1 %collective-permute-start.13 = (bf16[256,512]{1,0:T(8,128)(2,1)S(1)}, bf16[256,512]{1,0:T(8,128)(2,1)S(1)}, u32[]{:S(2)}, u32[]{:S(2)}) collective-permute-start(bf16[256,512]{1,0:T(8,128)(2,1)S(1)} %get-tuple-element.122), channel_id=1, source_target_pairs={{4,0},{6,2},{8,4},{10,6},{12,8},{14,10},{5,1},{7,3},{9,5},{11,7},{... | collective-permute-start | bytes 786440 | tf_op jit(solution)/shard_map/ppermute | solution.py:45
  90.9 13.9 %collective-permute-start.14 = (bf16[256,512]{1,0:T(8,128)(2,1)S(1)}, bf16[256,512]{1,0:T(8,128)(2,1)S(1)}, u32[]{:S(2)}, u32[]{:S(2)}) collective-permute-start(bf16[256,512]{1,0:T(8,128)(2,1)S(1)} %get-tuple-element.122), channel_id=1, source_target_pairs={{6,0},{4,2},{10,4},{8,6},{14,8},{12,10},{7,1},{5,3},{11,5},{9,7},{... | collective-permute-start | bytes 786440 | tf_op jit(solution)/shard_map/ppermute | solution.py:45
  105.5 29.8 %collective-permute-start.15 = (bf16[256,512]{1,0:T(8,128)(2,1)S(1)}, bf16[256,512]{1,0:T(8,128)(2,1)S(1)}, u32[]{:S(2)}, u32[]{:S(2)}) collective-permute-start(bf16[256,512]{1,0:T(8,128)(2,1)S(1)} %get-tuple-element.123), channel_id=1, source_target_pairs={{0,4},{2,6},{4,8},{6,10},{8,12},{10,14},{1,5},{3,7},{5,9},{7,11},{... | collective-permute-start | bytes 786440 | tf_op jit(solution)/shard_map/ppermute | solution.py:45
  107.7 32.5 %collective-permute-start.16 = (bf16[256,512]{1,0:T(8,128)(2,1)S(1)}, bf16[256,512]{1,0:T(8,128)(2,1)S(1)}, u32[]{:S(2)}, u32[]{:S(2)}) collective-permute-start(bf16[256,512]{1,0:T(8,128)(2,1)S(1)} %get-tuple-element.123), channel_id=1, source_target_pairs={{2,4},{0,6},{6,8},{4,10},{10,12},{8,14},{3,5},{1,7},{7,9},{5,11},{... | collective-permute-start | bytes 786440 | tf_op jit(solution)/shard_map/ppermute | solution.py:45
  128.5 18.4 %collective-permute-start.17 = (bf16[256,512]{1,0:T(8,128)(2,1)S(1)}, bf16[256,512]{1,0:T(8,128)(2,1)S(1)}, u32[]{:S(2)}, u32[]{:S(2)}) collective-permute-start(bf16[256,512]{1,0:T(8,128)(2,1)S(1)} %get-tuple-element.123), channel_id=1, source_target_pairs={{2,0},{0,2},{6,4},{4,6},{10,8},{8,10},{14,12},{12,14},{3,1},{1,3},... | collective-permute-start | bytes 786440 | tf_op jit(solution)/shard_map/ppermute | solution.py:45
  129.1 18.5 %collective-permute-start.18 = (bf16[256,512]{1,0:T(8,128)(2,1)S(1)}, bf16[256,512]{1,0:T(8,128)(2,1)S(1)}, u32[]{:S(2)}, u32[]{:S(2)}) collective-permute-start(bf16[256,512]{1,0:T(8,128)(2,1)S(1)} %get-tuple-element.123), channel_id=1, source_target_pairs={{4,0},{6,2},{8,4},{10,6},{12,8},{14,10},{5,1},{7,3},{9,5},{11,7},{... | collective-permute-start | bytes 786440 | tf_op jit(solution)/shard_map/ppermute | solution.py:45
  132.5 15.8 %collective-permute-start.19 = (bf16[256,512]{1,0:T(8,128)(2,1)S(1)}, bf16[256,512]{1,0:T(8,128)(2,1)S(1)}, u32[]{:S(2)}, u32[]{:S(2)}) collective-permute-start(bf16[256,512]{1,0:T(8,128)(2,1)S(1)} %get-tuple-element.123), channel_id=1, source_target_pairs={{6,0},{4,2},{10,4},{8,6},{14,8},{12,10},{7,1},{5,3},{11,5},{9,7},{... | collective-permute-start | bytes 786440 | tf_op jit(solution)/shard_map/ppermute | solution.py:45
  149.1 0.7 copy-start.1
where the time goes:
time: 151 us; the launch traced here: 150 us
  starting transfers between devices  86.8 us (57%)
  waiting for transfers between devices  24.1 us (16%)
  local copies, waits for them, and re-layouts  18.5 us (12%)
  between operations  10.7 us (7%)
  other arithmetic  5.7 us (4%)
  matrix products  4 us (3%)
    ppermute x20, starting transfers between devices, neighbourhood(): pieces.append(lax.ppermute(local_block, ('space', 'blk'), pairs))  86.8 us
    ppermute x20, waiting for transfers between devices, neighbourhood(): pieces.append(lax.ppermute(local_block, ('space', 'blk'), pairs))  24.1 us
    unnamed x28, local copies, waits for them, and re-layouts  15 us
    dot_general x4, matrix products, body(): term = jnp.dot(values, coeff[0, j], preferred_element_type=jnp.float32)  3.7 us
  transfers between devices with their start and end apart: 20, of which 4 were waited for; matrix products, arithmetic and copies ran while one was open for 14% of the time, Pallas kernels for 0%

commit v1 on v0

--- a/solution.py
+++ b/solution.py
@@ -1,6 +1,10 @@
+import functools
+
 import jax
 import jax.numpy as jnp
 from jax import lax
+from jax.experimental import pallas as pl
+from jax.experimental.pallas import tpu as pltpu
 from jax.sharding import PartitionSpec as P
 
 LEVELS = 4
@@ -43,7 +47,61 @@
                 continue
             pairs = window_pairs(space_count, part_size, distance, offset)
             pieces.append(lax.ppermute(local_block, ("space", "blk"), pairs))
-    return jnp.stack(pieces, axis=0)
+    return pieces
+
+
+def mix_kernel(n_pieces, neigh, finish, pick_ref, use_ref, start_ref, coeff_ref, *rest):
+    if finish:
+        solve_ref, rest = rest[0], rest[1:]
+    pieces = rest[:n_pieces]
+    out_ref, values, acc, sems = rest[n_pieces:]
+    for j in range(neigh):
+        for p in range(n_pieces):
+
+            @pl.when((pick_ref[j] == p) & (use_ref[j] != 0))
+            def _():
+                pltpu.make_async_copy(pieces[p], values.at[j], sems.at[j]).start()
+
+    acc[...] = start_ref[...]
+    for j in range(neigh):
+
+        @pl.when(use_ref[j] != 0)
+        def _():
+            pltpu.make_async_copy(pieces[0], values.at[j], sems.at[j]).wait()
+            acc[...] -= jnp.dot(values[j], coeff_ref[j], preferred_element_type=jnp.float32)
+
+    if finish:
+        right_side = acc[...].astype(jnp.bfloat16)
+        out_ref[...] = jnp.dot(right_side, solve_ref[...], preferred_element_type=jnp.float32).astype(out_ref.dtype)
+    else:
+        out_ref[...] = acc[...]
+
+
+def mix(pick, use, start, coeff, pieces, solve=None):
+    neigh = coeff.shape[0]
+    rows, cols = start.shape
+    finish = solve is not None
+    vmem = pl.BlockSpec(memory_space=pltpu.VMEM)
+    smem = pl.BlockSpec(memory_space=pltpu.SMEM)
+    anywhere = pl.BlockSpec(memory_space=pl.ANY)
+    operands = [pick, use, start, coeff] + ([solve] if finish else []) + list(pieces)
+    in_specs = [smem, smem, vmem, vmem] + ([vmem] if finish else []) + [anywhere] * len(pieces)
+    out_dtype = jnp.bfloat16 if finish else jnp.float32
+    flops = 2 * rows * cols * coeff.shape[1] * (neigh + (1 if finish else 0))
+    return pl.pallas_call(
+        functools.partial(mix_kernel, len(pieces), neigh, finish),
+        out_shape=jax.ShapeDtypeStruct((rows, cols), out_dtype),
+        in_specs=in_specs,
+        out_specs=vmem,
+        scratch_shapes=[
+            pltpu.VMEM((neigh, rows, coeff.shape[1]), pieces[0].dtype),
+            pltpu.VMEM((rows, cols), jnp.float32),
+            pltpu.SemaphoreType.DMA((neigh,)),
+        ],
+        cost_estimate=pl.CostEstimate(
+            flops=flops, bytes_accessed=2 * (neigh + 1) * rows * cols * 4 + coeff.size * 2, transcendentals=0
+        ),
+    )(*operands)
 
 
 def body(coeff, solve, noise, prior, owner, nbrs):
@@ -52,46 +110,38 @@
     blk_index = lax.axis_index("blk")
     own_slot = space_index * part_size + blk_index
     count = owner.shape[0]
-    neigh = nbrs.shape[1]
     block_ids = jnp.arange(count, dtype=jnp.int32)
     levels = block_levels(nbrs, count)
     own_block = jnp.sum(jnp.where(owner == own_slot, block_ids, 0))
     own_level = jnp.sum(jnp.where(block_ids == own_block, levels, 0))
     own_list = jnp.sum(jnp.where((block_ids == own_block)[:, None], nbrs, 0), axis=0)
-    is_current = own_list >= count
+    is_current = (own_list >= count).astype(jnp.int32)
     target = jnp.remainder(own_list, count)
     near_slot = jnp.sum(jnp.where(target[:, None] == block_ids[None, :], owner[None, :], 0), axis=1)
     distance = near_slot // part_size - space_index
     offset = jnp.remainder(near_slot - blk_index, part_size)
-    piece = (distance + REACH) * part_size + offset
+    pick = ((distance + REACH) * part_size + offset).astype(jnp.int32)
 
-    prior_window = neighbourhood(prior[0])
-    start = noise[0]
-    for j in range(neigh):
-        values = lax.dynamic_index_in_dim(prior_window, piece[j], 0, keepdims=False)
-        term = jnp.dot(values, coeff[0, j], preferred_element_type=jnp.float32)
-        start = start - jnp.where(is_current[j], jnp.zeros_like(term), term)
+    prior_pieces = neighbourhood(prior[0])
+    start = mix(pick, 1 - is_current, noise[0], coeff[0], prior_pieces)
 
     current = jnp.zeros_like(prior[0])
-    window = None
+    pieces = None
     for level_now in range(LEVELS):
 
-        def compute_block(previous, window_now=window):
-            right_side = start
-            if window_now is not None:
-                for j in range(neigh):
-                    values = lax.dynamic_index_in_dim(window_now, piece[j], 0, keepdims=False)
-                    term = jnp.dot(values, coeff[0, j], preferred_element_type=jnp.float32)
-                    right_side = right_side - jnp.where(is_current[j], term, jnp.zeros_like(term))
-            result = jnp.dot(right_side.astype(jnp.bfloat16), solve[0], preferred_element_type=jnp.float32)
-            return result.astype(jnp.bfloat16)
+        def compute_block(previous, pieces_now=pieces):
+            if pieces_now is None:
+                right_side = start.astype(jnp.bfloat16)
+                result = jnp.dot(right_side, solve[0], preferred_element_type=jnp.float32)
+                return result.astype(jnp.bfloat16)
+            return mix(pick, is_current, start, coeff[0], pieces_now, solve[0])
 
         def unchanged(previous):
             return previous
 
         current = lax.cond(own_level == level_now, compute_block, unchanged, current)
         if level_now + 1 < LEVELS:
-            window = neighbourhood(current)
+            pieces = neighbourhood(current)
     return current[None]
 
 

time: 151 us -> 100 us (0.66)
  starting transfers between devices: 86.8 us -> 61.8 us
  local copies, waits for them, and re-layouts: 18.5 us -> 2.12 us
  between operations: 10.7 us -> 2.46 us
  Pallas kernels: 0 us -> 4.15 us
  matrix products: 4 us -> 0.3 us
  waiting for transfers between devices: 24.1 us -> 21.2 us
    ppermute x20, starting transfers between devices: 86.8 us -> 61.8 us  [neighbourhood(): pieces.append(lax.ppermute(local_block, ('space', 'blk'), pairs))]
    unnamed x28 -> x17, local copies, waits for them, and re-layouts: 15 us -> 2.12 us
    pallas_call x0 -> x1, Pallas kernels: none -> 4.15 us  [mix(): pl.pallas_call(functools.partial(mix_kernel, len(pieces), neigh, finish),...]
    dot_general x5 -> x1, matrix products: 4 us -> 0.3 us  [compute_block(): result = jnp.dot(right_side, solve[0], preferred_element_type=jnp.float32)]
    ppermute x20, waiting for transfers between devices: 24.1 us -> 21.2 us  [neighbourhood(): pieces.append(lax.ppermute(local_block, ('space', 'blk'), pairs))]
    another operation x4 -> x0, local copies, waits for them, and re-layouts: 2.16 us -> none  [neighbourhood(): return jnp.stack(pieces, axis=0)]
  transfers between devices with their start and end apart: 20 -> 20, of which waited for: 4 -> 9; matrix products, arithmetic and copies ran while one was open for 14% -> 7% of each run, Pallas kernels for 0% -> 0%
where the time goes in v1:
time: 100 us; the launch traced here: 98.2 us
  starting transfers between devices  61.8 us (62%)
  waiting for transfers between devices  21.2 us (21%)
  other arithmetic  6.12 us (6%)
  Pallas kernels  4.15 us (4%)
  between operations  2.46 us (2%)
  local copies, waits for them, and re-layouts  2.12 us (2%)
    ppermute x20, starting transfers between devices, neighbourhood(): pieces.append(lax.ppermute(local_block, ('space', 'blk'), pairs))  61.8 us
    ppermute x20, waiting for transfers between devices, neighbourhood(): pieces.append(lax.ppermute(local_block, ('space', 'blk'), pairs))  21.2 us
    pallas_call x1, Pallas kernels, mix(): pl.pallas_call(functools.partial(mix_kernel, len(pieces), neigh, finish),...  4.15 us
    unnamed x17, local copies, waits for them, and re-layouts  2.12 us
  transfers between devices with their start and end apart: 20, of which 9 were waited for; matrix products, arithmetic and copies ran while one was open for 7% of the time, Pallas kernels for 0%

profile of v1, /device:TPU:12, one launch (start us, length us, event | category | flops | bytes accessed | tf_op | source)
XLA Modules:
  0.0 98.2 jit_solution(12816340982064236361)
XLA Ops:
  0.0 3.3 %collective-permute-start.4 = (bf16[256,512]{1,0:T(8,128)(2,1)}, bf16[256,512]{1,0:T(8,128)(2,1)S(1)}, u32[]{:S(2)}, u32[]{:S(2)}) collective-permute-start(bf16[256,512]{1,0:T(8,128)(2,1)} %bitcast.24), channel_id=1, source_target_pairs={{6,0},{4,2},{10,4},{8,6},{14,8},{12,10},{7,1},{5,3},{11,5},{9,7},{... | collective-permute-start | bytes 786440 | tf_op jit(solution)/shard_map/ppermute | solution.py:49
  3.3 1.9 %collective-permute-start.3 = (bf16[256,512]{1,0:T(8,128)(2,1)}, bf16[256,512]{1,0:T(8,128)(2,1)S(1)}, u32[]{:S(2)}, u32[]{:S(2)}) collective-permute-start(bf16[256,512]{1,0:T(8,128)(2,1)} %bitcast.25), channel_id=1, source_target_pairs={{4,0},{6,2},{8,4},{10,6},{12,8},{14,10},{5,1},{7,3},{9,5},{11,7},{... | collective-permute-start | bytes 786440 | tf_op jit(solution)/shard_map/ppermute | solution.py:49
  5.2 0.6 collective-permute-start.2
  5.8 4.8 %collective-permute-start.1 = (bf16[256,512]{1,0:T(8,128)(2,1)}, bf16[256,512]{1,0:T(8,128)(2,1)S(1)}, u32[]{:S(2)}, u32[]{:S(2)}) collective-permute-start(bf16[256,512]{1,0:T(8,128)(2,1)} %bitcast.27), channel_id=1, source_target_pairs={{2,4},{0,6},{6,8},{4,10},{10,12},{8,14},{3,5},{1,7},{7,9},{5,11},{... | collective-permute-start | bytes 786440 | tf_op jit(solution)/shard_map/ppermute | solution.py:49
  10.7 3.5 %collective-permute-start = (bf16[256,512]{1,0:T(8,128)(2,1)}, bf16[256,512]{1,0:T(8,128)(2,1)S(1)}, u32[]{:S(2)}, u32[]{:S(2)}) collective-permute-start(bf16[256,512]{1,0:T(8,128)(2,1)} %bitcast.28), channel_id=1, source_target_pairs={{0,4},{2,6},{4,8},{6,10},{8,12},{10,14},{1,5},{3,7},{5,9},{7,11},{... | collective-permute-start | bytes 786440 | tf_op jit(solution)/shard_map/ppermute | solution.py:49
  14.2 1.3 %fusion.4 = s32[]{:T(128)} fusion(s32[8]{0:T(128)} %param.18, s32[]{:T(128)S(6)} %add.42), kind=kLoop, calls=%fused_computation.32 | loop fusion | flops 23 | bytes 40 | tf_op jit(solution)/shard_map/reduce_sum | solution.py:115
  15.5 0.6 iota_compare_fusion.2
  16.1 0.8 select_reduce_fusion.8
  16.9 0.5 broadcast_subtract_fusion
  17.5 0.8 select_reduce_fusion.3
  18.3 0.2 select_reduce_fusion.2
  18.6 0.2 select_reduce_fusion.1
  18.8 0.2 select_reduce_fusion
  19.0 1.2 %select_reduce_fusion.9 = s32[]{:T(128)} fusion(s32[8]{0:T(128)S(1)} %select_reduce_fusion.5, s32[]{:T(128)} %fusion.4), kind=kLoop, calls=%fused_computation.35 | loop fusion | flops 23 | bytes 40 | tf_op jit(solution)/shard_map/reduce_sum | solution.py:116
  20.9 0.0 collective-permute-done.4.rest_5_
  20.9 1.4 %collective-permute-done.2.rest_3_ = bf16[256,512]{1,0:T(8,128)(2,1)S(1)} collective-permute-done((bf16[256,512]{1,0:T(8,128)(2,1)}, bf16[256,512]{1,0:T(8,128)(2,1)S(1)}, u32[]{:S(2)}, u32[]{:S(2)}) %collective-permute-start.2) | collective-permute-done | bytes 262176 | tf_op jit(solution)/shard_map/ppermute | solution.py:49
  22.3 0.0 collective-permute-done.1.rest_1_
  22.3 0.4 collective-permute-done.rest_0_
  22.7 0.3 copy-done.5
  23.0 0.1 copy-done.6
  23.1 0.3 copy-done.7
  23.4 4.1 %shard_map.66 = f32[256,512]{1,0:T(8,128)S(1)} custom-call(s32[4]{0:T(128)S(1)} %fusion.3.pick_ref, s32[4]{0:T(128)} %get-tuple-element.132.use_ref, f32[256,512]{1,0:T(8,128)} %bitcast.23, bf16[4,512,512]{2,1,0:T(8,128)(2,1)} %bitcast.14, bf16[256,512]{1,0:T(8,128)(2,1)} %copy-done.7, bf16[256,512]{1,0:T(8,128)(2,1)} %copy-done.6, ...), custom_call_target="tpu_custom_call" | custom-call | flops 536870912 | bytes 7340032 | tf_op jit(solution)/shard_map/pallas_call | solution.py:91
  27.5 0.3 conditional.4
  27.6 0.3 convolution_convert_fusion
  27.9 1.9 %collective-permute-start.9 = (bf16[256,512]{1,0:T(8,128)(2,1)S(1)}, bf16[256,512]{1,0:T(8,128)(2,1)}, u32[]{:S(2)}, u32[]{:S(2)}) collective-permute-start(bf16[256,512]{1,0:T(8,128)(2,1)S(1)} %get-tuple-element.147), channel_id=1, source_target_pairs={{6,0},{4,2},{10,4},{8,6},{14,8},{12,10},{7,1},{5,3},{11,5},{9,7},{... | collective-permute-start | bytes 786440 | tf_op jit(solution)/shard_map/ppermute | solution.py:49
  29.8 1.9 %collective-permute-start.8 = (bf16[256,512]{1,0:T(8,128)(2,1)S(1)}, bf16[256,512]{1,0:T(8,128)(2,1)}, u32[]{:S(2)}, u32[]{:S(2)}) collective-permute-start(bf16[256,512]{1,0:T(8,128)(2,1)S(1)} %get-tuple-element.147), channel_id=1, source_target_pairs={{4,0},{6,2},{8,4},{10,6},{12,8},{14,10},{5,1},{7,3},{9,5},{11,7},{... | collective-permute-start | bytes 786440 | tf_op jit(solution)/shard_map/ppermute | solution.py:49
  31.7 0.6 collective-permute-start.7
  32.3 4.8 %collective-permute-start.6 = (bf16[256,512]{1,0:T(8,128)(2,1)S(1)}, bf16[256,512]{1,0:T(8,128)(2,1)}, u32[]{:S(2)}, u32[]{:S(2)}) collective-permute-start(bf16[256,512]{1,0:T(8,128)(2,1)S(1)} %get-tuple-element.147), channel_id=1, source_target_pairs={{2,4},{0,6},{6,8},{4,10},{10,12},{8,14},{3,5},{1,7},{7,9},{5,11},{... | collective-permute-start | bytes 786440 | tf_op jit(solution)/shard_map/ppermute | solution.py:49
  37.2 4.9 %collective-permute-start.5 = (bf16[256,512]{1,0:T(8,128)(2,1)S(1)}, bf16[256,512]{1,0:T(8,128)(2,1)}, u32[]{:S(2)}, u32[]{:S(2)}) collective-permute-start(bf16[256,512]{1,0:T(8,128)(2,1)S(1)} %get-tuple-element.147), channel_id=1, source_target_pairs={{0,4},{2,6},{4,8},{6,10},{8,12},{10,14},{1,5},{3,7},{5,9},{7,11},{... | collective-permute-start | bytes 786440 | tf_op jit(solution)/shard_map/ppermute | solution.py:49
  42.6 0.7 collective-permute-done.8
  43.3 6.7 %collective-permute-done.7 = bf16[256,512]{1,0:T(8,128)(2,1)} collective-permute-done((bf16[256,512]{1,0:T(8,128)(2,1)S(1)}, bf16[256,512]{1,0:T(8,128)(2,1)}, u32[]{:S(2)}, u32[]{:S(2)}) %collective-permute-start.7) | collective-permute-done | bytes 262176 | tf_op jit(solution)/shard_map/ppermute | solution.py:49
  50.0 1.9 %collective-permute-start.14 = (bf16[256,512]{1,0:T(8,128)(2,1)S(1)}, bf16[256,512]{1,0:T(8,128)(2,1)}, u32[]{:S(2)}, u32[]{:S(2)}) collective-permute-start(bf16[256,512]{1,0:T(8,128)(2,1)S(1)} %get-tuple-element.148), channel_id=1, source_target_pairs={{6,0},{4,2},{10,4},{8,6},{14,8},{12,10},{7,1},{5,3},{11,5},{9,7},{... | collective-permute-start | bytes 786440 | tf_op jit(solution)/shard_map/ppermute | solution.py:49
  52.0 2.7 %collective-permute-start.13 = (bf16[256,512]{1,0:T(8,128)(2,1)S(1)}, bf16[256,512]{1,0:T(8,128)(2,1)}, u32[]{:S(2)}, u32[]{:S(2)}) collective-permute-start(bf16[256,512]{1,0:T(8,128)(2,1)S(1)} %get-tuple-element.148), channel_id=1, source_target_pairs={{4,0},{6,2},{8,4},{10,6},{12,8},{14,10},{5,1},{7,3},{9,5},{11,7},{... | collective-permute-start | bytes 786440 | tf_op jit(solution)/shard_map/ppermute | solution.py:49
  54.7 3.3 %collective-permute-start.12 = (bf16[256,512]{1,0:T(8,128)(2,1)S(1)}, bf16[256,512]{1,0:T(8,128)(2,1)}, u32[]{:S(2)}, u32[]{:S(2)}) collective-permute-start(bf16[256,512]{1,0:T(8,128)(2,1)S(1)} %get-tuple-element.148), channel_id=1, source_target_pairs={{2,0},{0,2},{6,4},{4,6},{10,8},{8,10},{14,12},{12,14},{3,1},{1,3},... | collective-permute-start | bytes 786440 | tf_op jit(solution)/shard_map/ppermute | solution.py:49
  58.0 4.8 %collective-permute-start.11 = (bf16[256,512]{1,0:T(8,128)(2,1)S(1)}, bf16[256,512]{1,0:T(8,128)(2,1)}, u32[]{:S(2)}, u32[]{:S(2)}) collective-permute-start(bf16[256,512]{1,0:T(8,128)(2,1)S(1)} %get-tuple-element.148), channel_id=1, source_target_pairs={{2,4},{0,6},{6,8},{4,10},{10,12},{8,14},{3,5},{1,7},{7,9},{5,11},{... | collective-permute-start | bytes 786440 | tf_op jit(solution)/shard_map/ppermute | solution.py:49
  62.8 4.6 %collective-permute-start.10 = (bf16[256,512]{1,0:T(8,128)(2,1)S(1)}, bf16[256,512]{1,0:T(8,128)(2,1)}, u32[]{:S(2)}, u32[]{:S(2)}) collective-permute-start(bf16[256,512]{1,0:T(8,128)(2,1)S(1)} %get-tuple-element.148), channel_id=1, source_target_pairs={{0,4},{2,6},{4,8},{6,10},{8,12},{10,14},{1,5},{3,7},{5,9},{7,11},{... | collective-permute-start | bytes 786440 | tf_op jit(solution)/shard_map/ppermute | solution.py:49
  67.9 1.2 %collective-permute-done.13 = bf16[256,512]{1,0:T(8,128)(2,1)} collective-permute-done((bf16[256,512]{1,0:T(8,128)(2,1)S(1)}, bf16[256,512]{1,0:T(8,128)(2,1)}, u32[]{:S(2)}, u32[]{:S(2)}) %collective-permute-start.13) | collective-permute-done | bytes 262176 | tf_op jit(solution)/shard_map/ppermute | solution.py:49
  69.2 4.4 %collective-permute-done.12 = bf16[256,512]{1,0:T(8,128)(2,1)} collective-permute-done((bf16[256,512]{1,0:T(8,128)(2,1)S(1)}, bf16[256,512]{1,0:T(8,128)(2,1)}, u32[]{:S(2)}, u32[]{:S(2)}) %collective-permute-start.12) | collective-permute-done | bytes 262176 | tf_op jit(solution)/shard_map/ppermute | solution.py:49
  73.6 1.2 %collective-permute-done.10 = bf16[256,512]{1,0:T(8,128)(2,1)} collective-permute-done((bf16[256,512]{1,0:T(8,128)(2,1)S(1)}, bf16[256,512]{1,0:T(8,128)(2,1)}, u32[]{:S(2)}, u32[]{:S(2)}) %collective-permute-start.10) | collective-permute-done | bytes 262176 | tf_op jit(solution)/shard_map/ppermute | solution.py:49
  74.8 1.9 %collective-permute-start.19 = (bf16[256,512]{1,0:T(8,128)(2,1)S(1)}, bf16[256,512]{1,0:T(8,128)(2,1)}, u32[]{:S(2)}, u32[]{:S(2)}) collective-permute-start(bf16[256,512]{1,0:T(8,128)(2,1)S(1)} %get-tuple-element.149), channel_id=1, source_target_pairs={{6,0},{4,2},{10,4},{8,6},{14,8},{12,10},{7,1},{5,3},{11,5},{9,7},{... | collective-permute-start | bytes 786440 | tf_op jit(solution)/shard_map/ppermute | solution.py:49
  76.7 1.9 %collective-permute-start.18 = (bf16[256,512]{1,0:T(8,128)(2,1)S(1)}, bf16[256,512]{1,0:T(8,128)(2,1)}, u32[]{:S(2)}, u32[]{:S(2)}) collective-permute-start(bf16[256,512]{1,0:T(8,128)(2,1)S(1)} %get-tuple-element.149), channel_id=1, source_target_pairs={{4,0},{6,2},{8,4},{10,6},{12,8},{14,10},{5,1},{7,3},{9,5},{11,7},{... | collective-permute-start | bytes 786440 | tf_op jit(solution)/shard_map/ppermute | solution.py:49
  78.6 1.5 %collective-permute-start.17 = (bf16[256,512]{1,0:T(8,128)(2,1)S(1)}, bf16[256,512]{1,0:T(8,128)(2,1)}, u32[]{:S(2)}, u32[]{:S(2)}) collective-permute-start(bf16[256,512]{1,0:T(8,128)(2,1)S(1)} %get-tuple-element.149), channel_id=1, source_target_pairs={{2,0},{0,2},{6,4},{4,6},{10,8},{8,10},{14,12},{12,14},{3,1},{1,3},... | collective-permute-start | bytes 786440 | tf_op jit(solution)/shard_map/ppermute | solution.py:49
  80.1 6.3 %collective-permute-start.16 = (bf16[256,512]{1,0:T(8,128)(2,1)S(1)}, bf16[256,512]{1,0:T(8,128)(2,1)}, u32[]{:S(2)}, u32[]{:S(2)}) collective-permute-start(bf16[256,512]{1,0:T(8,128)(2,1)S(1)} %get-tuple-element.149), channel_id=1, source_target_pairs={{2,4},{0,6},{6,8},{4,10},{10,12},{8,14},{3,5},{1,7},{7,9},{5,11},{... | collective-permute-start | bytes 786440 | tf_op jit(solution)/shard_map/ppermute | solution.py:49
  86.5 4.6 %collective-permute-start.15 = (bf16[256,512]{1,0:T(8,128)(2,1)S(1)}, bf16[256,512]{1,0:T(8,128)(2,1)}, u32[]{:S(2)}, u32[]{:S(2)}) collective-permute-start(bf16[256,512]{1,0:T(8,128)(2,1)S(1)} %get-tuple-element.149), channel_id=1, source_target_pairs={{0,4},{2,6},{4,8},{6,10},{8,12},{10,14},{1,5},{3,7},{5,9},{7,11},{... | collective-permute-start | bytes 786440 | tf_op jit(solution)/shard_map/ppermute | solution.py:49
  91.6 0.7 copy.22
  92.3 4.0 %collective-permute-done.17 = bf16[256,512]{1,0:T(8,128)(2,1)} collective-permute-done((bf16[256,512]{1,0:T(8,128)(2,1)S(1)}, bf16[256,512]{1,0:T(8,128)(2,1)}, u32[]{:S(2)}, u32[]{:S(2)}) %collective-permute-start.17) | collective-permute-done | bytes 262176 | tf_op jit(solution)/shard_map/ppermute | solution.py:49
  96.3 1.2 %collective-permute-done.15 = bf16[256,512]{1,0:T(8,128)(2,1)} collective-permute-done((bf16[256,512]{1,0:T(8,128)(2,1)S(1)}, bf16[256,512]{1,0:T(8,128)(2,1)}, u32[]{:S(2)}, u32[]{:S(2)}) %collective-permute-start.15) | collective-permute-done | bytes 262176 | tf_op jit(solution)/shard_map/ppermute | solution.py:49
  97.5 0.7 copy-done.2
  (29 shorter events, 0.2 us)
Async XLA Ops:
  0.0 20.9 %collective-permute-start.4 = (bf16[256,512]{1,0:T(8,128)(2,1)}, bf16[256,512]{1,0:T(8,128)(2,1)S(1)}, u32[]{:S(2)}, u32[]{:S(2)}) collective-permute-start(bf16[256,512]{1,0:T(8,128)(2,1)} %bitcast.24), channel_id=1, source_target_pairs={{6,0},{4,2},{10,4},{8,6},{14,8},{12,10},{7,1},{5,3},{11,5},{9,7},{... | collective-permute-start | bytes 786440 | tf_op jit(solution)/shard_map/ppermute | solution.py:49
  3.3 17.6 %collective-permute-start.3 = (bf16[256,512]{1,0:T(8,128)(2,1)}, bf16[256,512]{1,0:T(8,128)(2,1)S(1)}, u32[]{:S(2)}, u32[]{:S(2)}) collective-permute-start(bf16[256,512]{1,0:T(8,128)(2,1)} %bitcast.25), channel_id=1, source_target_pairs={{4,0},{6,2},{8,4},{10,6},{12,8},{14,10},{5,1},{7,3},{9,5},{11,7},{... | collective-permute-start | bytes 786440 | tf_op jit(solution)/shard_map/ppermute | solution.py:49
  5.2 17.1 %collective-permute-start.2 = (bf16[256,512]{1,0:T(8,128)(2,1)}, bf16[256,512]{1,0:T(8,128)(2,1)S(1)}, u32[]{:S(2)}, u32[]{:S(2)}) collective-permute-start(bf16[256,512]{1,0:T(8,128)(2,1)} %bitcast.26), channel_id=1, source_target_pairs={{2,0},{0,2},{6,4},{4,6},{10,8},{8,10},{14,12},{12,14},{3,1},{1,3},... | collective-permute-start | bytes 786440 | tf_op jit(solution)/shard_map/ppermute | solution.py:49
  5.8 16.5 %collective-permute-start.1 = (bf16[256,512]{1,0:T(8,128)(2,1)}, bf16[256,512]{1,0:T(8,128)(2,1)S(1)}, u32[]{:S(2)}, u32[]{:S(2)}) collective-permute-start(bf16[256,512]{1,0:T(8,128)(2,1)} %bitcast.27), channel_id=1, source_target_pairs={{2,4},{0,6},{6,8},{4,10},{10,12},{8,14},{3,5},{1,7},{7,9},{5,11},{... | collective-permute-start | bytes 786440 | tf_op jit(solution)/shard_map/ppermute | solution.py:49
  10.7 12.0 %collective-permute-start = (bf16[256,512]{1,0:T(8,128)(2,1)}, bf16[256,512]{1,0:T(8,128)(2,1)S(1)}, u32[]{:S(2)}, u32[]{:S(2)}) collective-permute-start(bf16[256,512]{1,0:T(8,128)(2,1)} %bitcast.28), channel_id=1, source_target_pairs={{0,4},{2,6},{4,8},{6,10},{8,12},{10,14},{1,5},{3,7},{5,9},{7,11},{... | collective-permute-start | bytes 786440 | tf_op jit(solution)/shard_map/ppermute | solution.py:49
  20.9 2.5 %copy-start.3 = (bf16[256,512]{1,0:T(8,128)(2,1)}, bf16[256,512]{1,0:T(8,128)(2,1)S(1)}, u32[]{:S(2)}) copy-start(bf16[256,512]{1,0:T(8,128)(2,1)S(1)} %collective-permute-done.4.rest_5_) | copy-start | bytes 786436
  20.9 1.8 %copy-start.4 = (bf16[256,512]{1,0:T(8,128)(2,1)}, bf16[256,512]{1,0:T(8,128)(2,1)S(1)}, u32[]{:S(2)}) copy-start(bf16[256,512]{1,0:T(8,128)(2,1)S(1)} %collective-permute-done.3.rest_4_) | copy-start | bytes 786436
  22.3 0.7 copy-start.5
  22.3 0.8 copy-start.6
  22.7 0.7 copy-start.7
  23.4 4.2 %copy-start.1 = (bf16[1,512,512]{2,1,0:T(8,128)(2,1)S(1)}, bf16[1,512,512]{2,1,0:T(8,128)(2,1)}, u32[]{:S(2)}) copy-start(bf16[1,512,512]{2,1,0:T(8,128)(2,1)} %param.15) | copy-start | bytes 1572868
  23.4 26.6 %copy-start = (bf16[1,4,512,512]{3,2,1,0:T(8,128)(2,1)S(1)}, bf16[1,4,512,512]{3,2,1,0:T(8,128)(2,1)}, u32[]{:S(2)}) copy-start(bf16[1,4,512,512]{3,2,1,0:T(8,128)(2,1)} %param.14) | copy-start | bytes 6291460
  27.9 14.7 %collective-permute-start.9 = (bf16[256,512]{1,0:T(8,128)(2,1)S(1)}, bf16[256,512]{1,0:T(8,128)(2,1)}, u32[]{:S(2)}, u32[]{:S(2)}) collective-permute-start(bf16[256,512]{1,0:T(8,128)(2,1)S(1)} %get-tuple-element.147), channel_id=1, source_target_pairs={{6,0},{4,2},{10,4},{8,6},{14,8},{12,10},{7,1},{5,3},{11,5},{9,7},{... | collective-permute-start | bytes 786440 | tf_op jit(solution)/shard_map/ppermute | solution.py:49
  29.8 13.5 %collective-permute-start.8 = (bf16[256,512]{1,0:T(8,128)(2,1)S(1)}, bf16[256,512]{1,0:T(8,128)(2,1)}, u32[]{:S(2)}, u32[]{:S(2)}) collective-permute-start(bf16[256,512]{1,0:T(8,128)(2,1)S(1)} %get-tuple-element.147), channel_id=1, source_target_pairs={{4,0},{6,2},{8,4},{10,6},{12,8},{14,10},{5,1},{7,3},{9,5},{11,7},{... | collective-permute-start | bytes 786440 | tf_op jit(solution)/shard_map/ppermute | solution.py:49
  31.7 18.3 %collective-permute-start.7 = (bf16[256,512]{1,0:T(8,128)(2,1)S(1)}, bf16[256,512]{1,0:T(8,128)(2,1)}, u32[]{:S(2)}, u32[]{:S(2)}) collective-permute-start(bf16[256,512]{1,0:T(8,128)(2,1)S(1)} %get-tuple-element.147), channel_id=1, source_target_pairs={{2,0},{0,2},{6,4},{4,6},{10,8},{8,10},{14,12},{12,14},{3,1},{1,3},... | collective-permute-start | bytes 786440 | tf_op jit(solution)/shard_map/ppermute | solution.py:49
  32.3 17.7 %collective-permute-start.6 = (bf16[256,512]{1,0:T(8,128)(2,1)S(1)}, bf16[256,512]{1,0:T(8,128)(2,1)}, u32[]{:S(2)}, u32[]{:S(2)}) collective-permute-start(bf16[256,512]{1,0:T(8,128)(2,1)S(1)} %get-tuple-element.147), channel_id=1, source_target_pairs={{2,4},{0,6},{6,8},{4,10},{10,12},{8,14},{3,5},{1,7},{7,9},{5,11},{... | collective-permute-start | bytes 786440 | tf_op jit(solution)/shard_map/ppermute | solution.py:49
  37.2 12.8 %collective-permute-start.5 = (bf16[256,512]{1,0:T(8,128)(2,1)S(1)}, bf16[256,512]{1,0:T(8,128)(2,1)}, u32[]{:S(2)}, u32[]{:S(2)}) collective-permute-start(bf16[256,512]{1,0:T(8,128)(2,1)S(1)} %get-tuple-element.147), channel_id=1, source_target_pairs={{0,4},{2,6},{4,8},{6,10},{8,12},{10,14},{1,5},{3,7},{5,9},{7,11},{... | collective-permute-start | bytes 786440 | tf_op jit(solution)/shard_map/ppermute | solution.py:49
  50.0 17.9 %collective-permute-start.14 = (bf16[256,512]{1,0:T(8,128)(2,1)S(1)}, bf16[256,512]{1,0:T(8,128)(2,1)}, u32[]{:S(2)}, u32[]{:S(2)}) collective-permute-start(bf16[256,512]{1,0:T(8,128)(2,1)S(1)} %get-tuple-element.148), channel_id=1, source_target_pairs={{6,0},{4,2},{10,4},{8,6},{14,8},{12,10},{7,1},{5,3},{11,5},{9,7},{... | collective-permute-start | bytes 786440 | tf_op jit(solution)/shard_map/ppermute | solution.py:49
  52.0 17.2 %collective-permute-start.13 = (bf16[256,512]{1,0:T(8,128)(2,1)S(1)}, bf16[256,512]{1,0:T(8,128)(2,1)}, u32[]{:S(2)}, u32[]{:S(2)}) collective-permute-start(bf16[256,512]{1,0:T(8,128)(2,1)S(1)} %get-tuple-element.148), channel_id=1, source_target_pairs={{4,0},{6,2},{8,4},{10,6},{12,8},{14,10},{5,1},{7,3},{9,5},{11,7},{... | collective-permute-start | bytes 786440 | tf_op jit(solution)/shard_map/ppermute | solution.py:49
  54.7 18.9 %collective-permute-start.12 = (bf16[256,512]{1,0:T(8,128)(2,1)S(1)}, bf16[256,512]{1,0:T(8,128)(2,1)}, u32[]{:S(2)}, u32[]{:S(2)}) collective-permute-start(bf16[256,512]{1,0:T(8,128)(2,1)S(1)} %get-tuple-element.148), channel_id=1, source_target_pairs={{2,0},{0,2},{6,4},{4,6},{10,8},{8,10},{14,12},{12,14},{3,1},{1,3},... | collective-permute-start | bytes 786440 | tf_op jit(solution)/shard_map/ppermute | solution.py:49
  58.0 15.6 %collective-permute-start.11 = (bf16[256,512]{1,0:T(8,128)(2,1)S(1)}, bf16[256,512]{1,0:T(8,128)(2,1)}, u32[]{:S(2)}, u32[]{:S(2)}) collective-permute-start(bf16[256,512]{1,0:T(8,128)(2,1)S(1)} %get-tuple-element.148), channel_id=1, source_target_pairs={{2,4},{0,6},{6,8},{4,10},{10,12},{8,14},{3,5},{1,7},{7,9},{5,11},{... | collective-permute-start | bytes 786440 | tf_op jit(solution)/shard_map/ppermute | solution.py:49
  62.8 11.9 %collective-permute-start.10 = (bf16[256,512]{1,0:T(8,128)(2,1)S(1)}, bf16[256,512]{1,0:T(8,128)(2,1)}, u32[]{:S(2)}, u32[]{:S(2)}) collective-permute-start(bf16[256,512]{1,0:T(8,128)(2,1)S(1)} %get-tuple-element.148), channel_id=1, source_target_pairs={{0,4},{2,6},{4,8},{6,10},{8,12},{10,14},{1,5},{3,7},{5,9},{7,11},{... | collective-permute-start | bytes 786440 | tf_op jit(solution)/shard_map/ppermute | solution.py:49
  74.8 17.5 %collective-permute-start.19 = (bf16[256,512]{1,0:T(8,128)(2,1)S(1)}, bf16[256,512]{1,0:T(8,128)(2,1)}, u32[]{:S(2)}, u32[]{:S(2)}) collective-permute-start(bf16[256,512]{1,0:T(8,128)(2,1)S(1)} %get-tuple-element.149), channel_id=1, source_target_pairs={{6,0},{4,2},{10,4},{8,6},{14,8},{12,10},{7,1},{5,3},{11,5},{9,7},{... | collective-permute-start | bytes 786440 | tf_op jit(solution)/shard_map/ppermute | solution.py:49
  76.7 15.6 %collective-permute-start.18 = (bf16[256,512]{1,0:T(8,128)(2,1)S(1)}, bf16[256,512]{1,0:T(8,128)(2,1)}, u32[]{:S(2)}, u32[]{:S(2)}) collective-permute-start(bf16[256,512]{1,0:T(8,128)(2,1)S(1)} %get-tuple-element.149), channel_id=1, source_target_pairs={{4,0},{6,2},{8,4},{10,6},{12,8},{14,10},{5,1},{7,3},{9,5},{11,7},{... | collective-permute-start | bytes 786440 | tf_op jit(solution)/shard_map/ppermute | solution.py:49
  78.6 17.6 %collective-permute-start.17 = (bf16[256,512]{1,0:T(8,128)(2,1)S(1)}, bf16[256,512]{1,0:T(8,128)(2,1)}, u32[]{:S(2)}, u32[]{:S(2)}) collective-permute-start(bf16[256,512]{1,0:T(8,128)(2,1)S(1)} %get-tuple-element.149), channel_id=1, source_target_pairs={{2,0},{0,2},{6,4},{4,6},{10,8},{8,10},{14,12},{12,14},{3,1},{1,3},... | collective-permute-start | bytes 786440 | tf_op jit(solution)/shard_map/ppermute | solution.py:49
  80.1 16.2 %collective-permute-start.16 = (bf16[256,512]{1,0:T(8,128)(2,1)S(1)}, bf16[256,512]{1,0:T(8,128)(2,1)}, u32[]{:S(2)}, u32[]{:S(2)}) collective-permute-start(bf16[256,512]{1,0:T(8,128)(2,1)S(1)} %get-tuple-element.149), channel_id=1, source_target_pairs={{2,4},{0,6},{6,8},{4,10},{10,12},{8,14},{3,5},{1,7},{7,9},{5,11},{... | collective-permute-start | bytes 786440 | tf_op jit(solution)/shard_map/ppermute | solution.py:49
  86.5 11.0 %collective-permute-start.15 = (bf16[256,512]{1,0:T(8,128)(2,1)S(1)}, bf16[256,512]{1,0:T(8,128)(2,1)}, u32[]{:S(2)}, u32[]{:S(2)}) collective-permute-start(bf16[256,512]{1,0:T(8,128)(2,1)S(1)} %get-tuple-element.149), channel_id=1, source_target_pairs={{0,4},{2,6},{4,8},{6,10},{8,12},{10,14},{1,5},{3,7},{5,9},{7,11},{... | collective-permute-start | bytes 786440 | tf_op jit(solution)/shard_map/ppermute | solution.py:49
  97.5 0.7 copy-start.2
